TPU v7x, 512 devices: a whole 4x8x8 slice. The times are simulated.
512 devices in a mesh: dp: 16 (over y, core), tensor: 32 (over z, x).
Axes of the slice: x: 4, y: 8, z: 8, core: 2. Of those that a mesh axis runs over, the one named last changes fastest.
Arguments:
- layer_input: bfloat16 [65536, 8192], P('dp', 'tensor'), may hold values from -6 to 6
- output_grad: bfloat16 [65536, 1024], P(('dp', 'tensor')), may hold values from -6 to 6
- key_weight: bfloat16 [8192, 1024], P('tensor'), may hold values from -0.0625 to 0.0625
- adapter_down: bfloat16 [128, 16, 8192], P('dp', None, 'tensor'), may hold values from -0.0625 to 0.0625
- adapter_up: bfloat16 [128, 16, 1024], P('dp', None, 'tensor'), may hold values from -0.1875 to 0.1875
- segment_adapter: int32 [512], replicated, may hold values from 0 to 127
- adapter_slot: int32 [128], replicated, may hold values from 0 to 127, each once
- live_segments: int32 [16], P('dp'), may hold values from 1 to 32, as said below
Outputs:
- input_grad: bfloat16 [65536, 8192], P('dp', 'tensor')
- down_grad: bfloat16 [128, 16, 8192], P('dp', None, 'tensor')
- up_grad: bfloat16 [128, 16, 1024], P('dp', None, 'tensor')
Inputs may be any that keep to these rules, and one draw needn't show every extreme that they name: `live_segments`: some data group has all 32 segments live; a group's segments at or past its count are padding.
All inputs are finite; a program needn't handle non-finite values.
Results may differ from a plain program's by a relative error of at most 0.0057.
Values may be sent and summed in bfloat16 or wider, within the bound.
No kernel may reach another device: no remote copies, remote signals or barrier semaphores. Data moves between devices by JAX's collectives and lax.ppermute only.
A program may use at most 64 MiB of HBM per device.

v0:
```python
import jax
import jax.numpy as jnp
from jax import lax
from jax.sharding import PartitionSpec as P


def on_device(
    layer_input,
    output_grad,
    key_weight,
    adapter_down,
    adapter_up,
    segment_adapter,
    adapter_slot,
    live_segments,
):
    tensor_size = lax.axis_size("tensor")
    position = lax.axis_index("tensor")
    group_count = lax.axis_size("dp")
    group_index = lax.axis_index("dp")
    row_count = output_grad.shape[0]
    tok_group = layer_input.shape[0]
    width_shard = layer_input.shape[1]
    key_width = output_grad.shape[1]
    key_shard = key_width // tensor_size
    adapters = adapter_slot.shape[0]
    rank_dim = adapter_down.shape[1]
    per_owner = adapter_down.shape[0]
    seg_total = segment_adapter.shape[0]
    seg_group = seg_total // group_count
    seg_len = tok_group // seg_group
    f32 = jnp.float32
    bf16 = jnp.bfloat16
    whole_raw = lax.all_gather(output_grad, "tensor", axis=0, tiled=True)
    slot_ids = jnp.arange(adapters, dtype=jnp.int32)
    lookup = segment_adapter[:, None] == slot_ids[None, :]
    every_slot = jnp.sum(jnp.where(lookup, adapter_slot[None, :], 0), axis=1)
    seg_slot = lax.dynamic_slice_in_dim(every_slot, group_index * seg_group, seg_group)
    seg_live = jnp.arange(seg_group, dtype=jnp.int32) < live_segments[0]
    local_store = jnp.concatenate([adapter_down, adapter_up], axis=2).reshape(per_owner, -1)
    spread = jnp.broadcast_to(local_store[None], (group_count,) + local_store.shape)
    stores = lax.all_to_all(spread, "dp", 0, 0, tiled=True).reshape(adapters, -1)
    choose = (seg_slot[:, None] == slot_ids[None, :]).astype(bf16)
    seg_store = jnp.dot(choose, stores, preferred_element_type=f32).astype(bf16)
    seg_store = seg_store.reshape(seg_group, rank_dim, width_shard + key_shard)
    down_seg = seg_store[:, :, :width_shard]
    up_seg = seg_store[:, :, width_shard:]
    input_seg = layer_input.reshape(seg_group, seg_len, width_shard)
    proj_part = jnp.einsum("sjd,srd->srj", input_seg, down_seg, preferred_element_type=f32)
    first = jnp.concatenate([proj_part, up_seg.astype(f32)], axis=2).reshape(seg_group, -1)
    first = lax.all_to_all(first, "tensor", 0, 0, tiled=True)
    first = first.reshape(tensor_size, rank_dim, seg_len + key_shard)
    projected_own = jnp.sum(first[:, :, :seg_len], axis=0).astype(bf16)
    up_own = jnp.transpose(first[:, :, seg_len:], (1, 0, 2)).reshape(rank_dim, key_width)
    up_own = up_own.astype(bf16)
    own_live = position < live_segments[0]
    masked_own = jnp.where(own_live, output_grad, jnp.zeros_like(output_grad))
    lowrank_own = lax.dot_general(
        up_own, masked_own, (((1,), (1,)), ((), ())), preferred_element_type=f32
    ).astype(bf16)
    seg_up_own = 2.0 * jnp.dot(projected_own, masked_own, preferred_element_type=f32)
    low_spread = jnp.broadcast_to(
        lowrank_own.reshape(1, row_count * rank_dim), (tensor_size, row_count * rank_dim)
    )
    up_pieces = jnp.transpose(
        seg_up_own.reshape(rank_dim, tensor_size, key_shard), (1, 0, 2)
    ).reshape(tensor_size, rank_dim * key_shard)
    up_round = lax.reduce_precision(up_pieces, exponent_bits=8, mantissa_bits=7)
    up_high = up_round.astype(bf16)
    up_low = (up_pieces - up_round).astype(bf16)
    second = jnp.concatenate([low_spread, up_high, up_low], axis=1)
    second = second.reshape(tensor_size, -1, 128)
    second = lax.all_to_all(second, "tensor", 0, 0, tiled=True).reshape(tensor_size, -1)
    lowrank = second[:, : row_count * rank_dim].reshape(seg_group, rank_dim, seg_len)
    piece = rank_dim * key_shard
    low_end = row_count * rank_dim
    seg_up = second[:, low_end : low_end + piece].astype(f32)
    seg_up = seg_up + second[:, low_end + piece :].astype(f32)
    seg_up = seg_up.reshape(seg_group, rank_dim, key_shard)
    seg_down = 2.0 * jnp.einsum("srj,sjd->srd", lowrank, input_seg, preferred_element_type=f32)
    seg_grad = jnp.concatenate([seg_down, seg_up], axis=2)
    onehot = (slot_ids[:, None] == seg_slot[None, :]).astype(bf16)
    grad_round = lax.reduce_precision(seg_grad, exponent_bits=8, mantissa_bits=7)
    grad_high = grad_round.astype(bf16)
    grad_low = (seg_grad - grad_round).astype(bf16)
    flat_high = grad_high.reshape(seg_group, -1)
    flat_low = grad_low.reshape(seg_group, -1)
    part = jnp.dot(onehot, flat_high, preferred_element_type=f32)
    part = part + jnp.dot(onehot, flat_low, preferred_element_type=f32)
    part = part.astype(bf16).reshape(group_count, per_owner, -1)
    gathered = lax.all_to_all(part, "dp", 0, 0, tiled=True)
    frozen = lax.dot_general(
        whole_raw, key_weight, (((1,), (1,)), ((), ())), preferred_element_type=f32
    )
    frozen = jnp.where(jnp.repeat(seg_live, seg_len)[:, None], frozen, jnp.zeros_like(frozen))
    extra = jnp.einsum("srj,srd->sjd", lowrank, down_seg, preferred_element_type=f32)
    input_grad = (frozen + 2.0 * extra.reshape(tok_group, width_shard)).astype(bf16)
    gathered, input_grad = lax.optimization_barrier((gathered, input_grad))
    total = jnp.sum(gathered.astype(f32), axis=0).reshape(per_owner, rank_dim, -1)
    down_grad = total[:, :, :width_shard].astype(bf16)
    up_grad = total[:, :, width_shard:].astype(bf16)
    return (input_grad, down_grad, up_grad)


def solution(mesh):
    in_specs = (
        P("dp", "tensor"),
        P(("dp", "tensor"), None),
        P("tensor", None),
        P("dp", None, "tensor"),
        P("dp", None, "tensor"),
        P(),
        P(),
        P("dp"),
    )
    out_specs = (P("dp", "tensor"), P("dp", None, "tensor"), P("dp", None, "tensor"))
    return jax.shard_map(
        on_device, mesh=mesh, in_specs=in_specs, out_specs=out_specs, check_vma=False
    )
```

profile of v0, /device:TPU:1, one launch (start us, length us, event | category | flops | bytes accessed | tf_op | source)
XLA Modules:
  0.0 147.1 jit_solution(13841824733136216324)
XLA Ops:
  7.2 0.7 all-gather.2.cloned.1.call-update
  7.9 0.9 pad_maximum_fusion.2
  9.0 1.1 broadcast_in_dim.55
  10.0 10.4 %all-to-all-start = ((bf16[16,8,4608]{2,1,0:T(8,128)(2,1)}), bf16[16,8,4608]{2,1,0:T(8,128)(2,1)S(1)}, u32[]{:S(2)}, u32[]{:S(2)}) async-start(bf16[16,8,4608]{2,1,0:T(8,128)(2,1)} %broadcast_in_dim.55), calls=%async_computation | async-start | bytes 2359296 | tf_op jit(solution)/shard_map/all_to_all | solution.py:42
  20.4 0.2 select_reduce_fusion
  20.7 30.3 %all-to-all-done = bf16[16,8,4608]{2,1,0:T(8,128)(2,1)S(1)} async-done(((bf16[16,8,4608]{2,1,0:T(8,128)(2,1)}), bf16[16,8,4608]{2,1,0:T(8,128)(2,1)S(1)}, u32[]{:S(2)}, u32[]{:S(2)}) %all-to-all-start) | async-done | bytes 1179680 | tf_op jit(solution)/shard_map/all_to_all | solution.py:42
  51.0 1.1 convolution_convert_fusion
  52.1 1.5 %reshape.65 = bf16[32,16,288]{2,1,0:T(8,128)(2,1)S(1)} reshape(bf16[32,4608]{1,0:T(8,128)(2,1)} %convolution_convert_fusion) | data formatting | bytes 589824 | tf_op jit(solution)/shard_map/reshape | solution.py:45
  53.7 0.6 fusion.10
  54.4 1.4 all_to_all.20
  55.8 11.1 %all-to-all-start.1 = ((f32[32,1,2560]{2,1,0:T(1,128)}), f32[32,1,2560]{2,1,0:T(1,128)S(1)}, u32[]{:S(2)}, u32[]{:S(2)}) async-start(f32[32,1,2560]{2,1,0:T(1,128)} %all_to_all.20), calls=%async_computation.1 | async-start | bytes 655360 | tf_op jit(solution)/shard_map/all_to_all | solution.py:51
  67.5 13.1 %all-to-all-done.1 = f32[32,1,2560]{2,1,0:T(1,128)S(1)} async-done(((f32[32,1,2560]{2,1,0:T(1,128)}), f32[32,1,2560]{2,1,0:T(1,128)S(1)}, u32[]{:S(2)}, u32[]{:S(2)}) %all-to-all-start.1) | async-done | bytes 327712 | tf_op jit(solution)/shard_map/all_to_all | solution.py:51
  80.6 0.8 reduce.1
  81.4 0.3 reshape.67
  81.7 0.2 convolution_multiply_fusion.2
  82.0 0.2 copy.25
  82.4 0.2 convert_element_type.55
  82.6 0.2 fusion.5
  82.8 16.6 %all_to_all.25 = bf16[32,24,128]{2,1,0:T(8,128)(2,1)S(1)} all-to-all(bf16[32,24,128]{2,1,0:T(8,128)(2,1)S(1)} %bitcast.45), channel_id=1, replica_groups=mesh['dp'=16,'tensor'=32] {'tensor'}, dimensions={0} | all-to-all | bytes 393216 | tf_op jit(solution)/shard_map/all_to_all | solution.py:73
  99.7 0.4 convolution_multiply_fusion.1
  100.2 0.3 concatenate.18
  100.6 0.4 fusion.8
  101.0 1.6 %fusion.1 = bf16[16,8,4608]{2,1,0:T(8,128)(2,1)} fusion(f32[128,4608]{1,0:T(8,128)S(1)} %fusion.8, f32[32,4608]{1,0:T(8,128)S(1)} %concatenate.18, s32[32]{0:T(128)S(1)} %dynamic_slice.3), kind=kOutput, calls=%fused_computation.2 | convolution fusion | flops 39374848 | bytes 4128896 | tf_op jit(solution)/shard_map/dot_general | solution.py:89
  102.6 5.5 %all-to-all-start.3 = ((bf16[16,8,4608]{2,1,0:T(8,128)(2,1)}), bf16[16,8,4608]{2,1,0:T(8,128)(2,1)S(1)}, u32[]{:S(2)}, u32[]{:S(2)}) async-start(bf16[16,8,4608]{2,1,0:T(8,128)(2,1)} %fusion.1), calls=%async_computation.3 | async-start | bytes 2359296 | tf_op jit(solution)/shard_map/all_to_all | solution.py:91
  108.2 3.7 %convolution_multiply_fusion = f32[32,128,256]{2,1,0:T(8,128)} fusion(bf16[32,16,128]{2,1,0:T(8,128)(2,1)S(1)} %bitcast.41, bf16[32,16,288]{2,1,0:T(8,128)(2,1)} %copy-done.1), kind=kOutput, calls=%fused_computation.7 | convolution fusion | flops 34603008 | bytes 4587520 | tf_op jit(solution)/shard_map/srj,srd->sjd/dot_general | solution.py:96
  111.8 13.0 %all-gather.2.cloned.1.call-done = bf16[4096,1024]{1,0:T(8,128)(2,1)} async-done(((bf16[128,1024]{1,0:T(8,128)(2,1)}), bf16[4096,1024]{1,0:T(8,128)(2,1)}) %all-gather.2.cloned.1.call-update) | async-done | bytes 8388624 | tf_op jit(solution)/shard_map/all_gather | solution.py:34
  124.9 7.1 %fusion.3 = bf16[4096,256]{1,0:T(8,128)(2,1)} fusion(f32[4096,256]{1,0:T(8,128)} %bitcast.39, bf16[4096,1024]{1,0:T(8,128)(2,1)} %all-gather.2.cloned.1.call-done, bf16[256,1024]{1,0:T(8,128)(2,1)} %param.10, pred[4096]{0:T(1024)(128)(4,1)S(1)} %broadcast_bitcast_fusion), kind=kOutput, calls=%fused_computation.6 | convolution fusion | flops 2150629376 | bytes 15208448 | tf_op jit(solution)/shard_map/dot_general | solution.py:92
  131.9 6.7 %all-to-all-done.3 = bf16[16,8,4608]{2,1,0:T(8,128)(2,1)S(1)} async-done(((bf16[16,8,4608]{2,1,0:T(8,128)(2,1)}), bf16[16,8,4608]{2,1,0:T(8,128)(2,1)S(1)}, u32[]{:S(2)}, u32[]{:S(2)}) %all-to-all-start.3) | async-done | bytes 1179680 | tf_op jit(solution)/shard_map/all_to_all | solution.py:91
  138.7 0.2 reduce
  138.8 0.2 reshape.76
  139.0 0.6 slice.46
  139.7 0.6 slice.47
  (36 shorter events, 1.2 us)
Async XLA Ops:
  7.2 46.5 %copy-start = (bf16[4096,256]{1,0:T(8,128)(2,1)S(1)}, bf16[4096,256]{1,0:T(8,128)(2,1)}, u32[]{:S(2)}) copy-start(bf16[4096,256]{1,0:T(8,128)(2,1)} %param.8) | copy-start | bytes 6291460
  7.2 13.2 %copy-start.5 = (s32[512]{0:T(512)S(1)}, s32[512]{0:T(512)}, u32[]{:S(2)}) copy-start(s32[512]{0:T(512)} %param.13) | copy-start | bytes 6148
  7.2 13.2 %copy-start.6 = (s32[128]{0:T(128)S(1)}, s32[128]{0:T(128)}, u32[]{:S(2)}) copy-start(s32[128]{0:T(128)} %param.14) | copy-start | bytes 1540
  7.2 117.7 %all-gather.2.cloned.1.call-start = ((), (), s32[]{:S(2)}) async-start(), calls=%async_computation.4 | async-start | bytes 8650752 | tf_op jit(solution)/shard_map/all_gather | solution.py:34
  10.0 41.0 %all-to-all-start = ((bf16[16,8,4608]{2,1,0:T(8,128)(2,1)}), bf16[16,8,4608]{2,1,0:T(8,128)(2,1)S(1)}, u32[]{:S(2)}, u32[]{:S(2)}) async-start(bf16[16,8,4608]{2,1,0:T(8,128)(2,1)} %broadcast_in_dim.55), calls=%async_computation | async-start | bytes 2359296 | tf_op jit(solution)/shard_map/all_to_all | solution.py:42
  53.6 2.2 %copy-start.1 = (bf16[32,16,288]{2,1,0:T(8,128)(2,1)}, bf16[32,16,288]{2,1,0:T(8,128)(2,1)S(1)}, u32[]{:S(2)}) copy-start(bf16[32,16,288]{2,1,0:T(8,128)(2,1)S(1)} %reshape.65) | copy-start | bytes 884740
  54.3 27.4 %copy-start.4 = (bf16[128,1024]{1,0:T(8,128)(2,1)S(1)}, bf16[128,1024]{1,0:T(8,128)(2,1)}, u32[]{:S(2)}) copy-start(bf16[128,1024]{1,0:T(8,128)(2,1)} %param.9) | copy-start | bytes 786436
  55.8 24.9 %all-to-all-start.1 = ((f32[32,1,2560]{2,1,0:T(1,128)}), f32[32,1,2560]{2,1,0:T(1,128)S(1)}, u32[]{:S(2)}, u32[]{:S(2)}) async-start(f32[32,1,2560]{2,1,0:T(1,128)} %all_to_all.20), calls=%async_computation.1 | async-start | bytes 655360 | tf_op jit(solution)/shard_map/all_to_all | solution.py:51
  99.5 0.6 copy-start.2
  101.0 7.1 %copy-start.3 = (bf16[4,8,16,128]{3,2,1,0:T(8,128)(2,1)S(1)}, bf16[4,8,16,128]{3,2,1,0:T(8,128)(2,1)}, u32[]{:S(2)}) copy-start(bf16[4,8,16,128]{3,2,1,0:T(8,128)(2,1)} %copy-done.2) | copy-start | bytes 393220
  102.6 36.1 %all-to-all-start.3 = ((bf16[16,8,4608]{2,1,0:T(8,128)(2,1)}), bf16[16,8,4608]{2,1,0:T(8,128)(2,1)S(1)}, u32[]{:S(2)}, u32[]{:S(2)}) async-start(bf16[16,8,4608]{2,1,0:T(8,128)(2,1)} %fusion.1), calls=%async_computation.3 | async-start | bytes 2359296 | tf_op jit(solution)/shard_map/all_to_all | solution.py:91
Sparse Core Ops, SparseCore 0:
  11.2 113.6 all-gather.1
where the time goes:
time: 148 us; the launch traced here: 147 us
  waiting for transfers between devices  63.8 us (43%)
  starting transfers between devices  27 us (18%)
  blocking collectives  16.6 us (11%)
  matrix products  15.2 us (10%)
  between operations  14.9 us (10%)
  local copies, waits for them, and re-layouts  7.34 us (5%)
  other arithmetic  2.28 us (2%)
    all_to_all x1, waiting for transfers between devices, on_device(): lax.all_to_all(spread, 'dp', 0, 0, tiled=True).reshape(adapters, -1)  30.3 us
    all_to_all x1, blocking collectives, on_device(): lax.all_to_all(second, 'tensor', 0, 0, tiled=True).reshape(tensor_size, -1)  16.6 us
    all_to_all x1, waiting for transfers between devices, on_device(): first = lax.all_to_all(first, 'tensor', 0, 0, tiled=True)  13.1 us
    all_gather x1, waiting for transfers between devices, on_device(): whole_raw = lax.all_gather(output_grad, 'tensor', axis=0, tiled=True)  13 us
    all_to_all x1, starting transfers between devices, on_device(): first = lax.all_to_all(first, 'tensor', 0, 0, tiled=True)  11.1 us
    all_to_all x1, starting transfers between devices, on_device(): lax.all_to_all(spread, 'dp', 0, 0, tiled=True).reshape(adapters, -1)  10.4 us
    dot_general x1, matrix products, on_device(): lax.dot_general(whole_raw, key_weight, (((1,), (1,)), ((), ())), preferre...  7.09 us
    all_to_all x1, waiting for transfers between devices, on_device(): gathered = lax.all_to_all(part, 'dp', 0, 0, tiled=True)  6.74 us
  transfers between devices with their start and end apart: 4, of which 4 were waited for; matrix products, arithmetic and copies ran while one was open for 15% of the time, Pallas kernels for 0%

commit v1 on v0

--- a/solution.py
+++ b/solution.py
@@ -31,7 +31,9 @@
     seg_len = tok_group // seg_group
     f32 = jnp.float32
     bf16 = jnp.bfloat16
-    whole_raw = lax.all_gather(output_grad, "tensor", axis=0, tiled=True)
+    whole_raw = jnp.concatenate(
+        lax.all_to_all(jnp.stack([output_grad] * lax.axis_size("tensor")), "tensor", 0, 0), axis=0
+    )
     slot_ids = jnp.arange(adapters, dtype=jnp.int32)
     lookup = segment_adapter[:, None] == slot_ids[None, :]
     every_slot = jnp.sum(jnp.where(lookup, adapter_slot[None, :], 0), axis=1)

time: 148 us -> 327 us (2.21)
  waiting for transfers between devices: 63.8 us -> 253 us
  between operations: 14.9 us -> 1.57 us
  starting transfers between devices: 27 us -> 31.4 us
  local copies, waits for them, and re-layouts: 7.34 us -> 11.6 us
    all_to_all x0 -> x1, waiting for transfers between devices: none -> 186 us  [on_device(): lax.all_to_all(jnp.stack([output_grad] * lax.axis_size('tensor')), 'tenso...]
    all_to_all x1, waiting for transfers between devices: 6.74 us -> 22.8 us  [on_device(): gathered = lax.all_to_all(part, 'dp', 0, 0, tiled=True)]
    all_gather x1 -> x0, waiting for transfers between devices: 13 us -> none  [on_device(): whole_raw = lax.all_gather(output_grad, 'tensor', axis=0, tiled=True)]
    all_to_all x0 -> x1, starting transfers between devices: none -> 4.97 us  [on_device(): lax.all_to_all(jnp.stack([output_grad] * lax.axis_size('tensor')), 'tenso...]
    another operation x1 -> x2, local copies, waits for them, and re-layouts: 0.17 us -> 4.46 us  [the longest x1 4.29 us: on_device(): jnp.stack([output_grad] * lax.axis_size('tensor'))]
  transfers between devices with their start and end apart: 4 -> 4, of which waited for: 4 -> 4; matrix products, arithmetic and copies ran while one was open for 15% -> 3% of each run, Pallas kernels for 0% -> 0%
where the time goes in v1:
time: 327 us; the launch traced here: 326 us
  waiting for transfers between devices  253 us (77%)
  starting transfers between devices  31.4 us (10%)
  blocking collectives  14.6 us (4%)
  matrix products  12 us (4%)
  local copies, waits for them, and re-layouts  11.6 us (4%)
    all_to_all x1, waiting for transfers between devices, on_device(): lax.all_to_all(jnp.stack([output_grad] * lax.axis_size('tensor')), 'tenso...  186 us
    all_to_all x1, waiting for transfers between devices, on_device(): lax.all_to_all(spread, 'dp', 0, 0, tiled=True).reshape(adapters, -1)  30.3 us
    all_to_all x1, waiting for transfers between devices, on_device(): gathered = lax.all_to_all(part, 'dp', 0, 0, tiled=True)  22.8 us
    all_to_all x1, blocking collectives, on_device(): lax.all_to_all(second, 'tensor', 0, 0, tiled=True).reshape(tensor_size, -1)  14.6 us
    all_to_all x1, waiting for transfers between devices, on_device(): first = lax.all_to_all(first, 'tensor', 0, 0, tiled=True)  13.1 us
    all_to_all x1, starting transfers between devices, on_device(): first = lax.all_to_all(first, 'tensor', 0, 0, tiled=True)  11.1 us
    all_to_all x1, starting transfers between devices, on_device(): lax.all_to_all(spread, 'dp', 0, 0, tiled=True).reshape(adapters, -1)  10.4 us
  transfers between devices with their start and end apart: 4, of which 4 were waited for; matrix products, arithmetic and copies ran while one was open for 3% of the time, Pallas kernels for 0%

profile of v1, /device:TPU:1, one launch (start us, length us, event | category | flops | bytes accessed | tf_op | source)
XLA Modules:
  0.0 326.1 jit_solution(9230412032509231447)
XLA Ops:
  0.7 1.0 pad_maximum_fusion.2
  1.8 1.1 broadcast_in_dim.55
  2.9 10.4 %all-to-all-start = ((bf16[16,8,4608]{2,1,0:T(8,128)(2,1)}), bf16[16,8,4608]{2,1,0:T(8,128)(2,1)S(1)}, u32[]{:S(2)}, u32[]{:S(2)}) async-start(bf16[16,8,4608]{2,1,0:T(8,128)(2,1)} %broadcast_in_dim.55), calls=%async_computation | async-start | bytes 2359296 | tf_op jit(solution)/shard_map/all_to_all | solution.py:44
  13.3 0.2 select_reduce_fusion
  13.6 30.3 %all-to-all-done = bf16[16,8,4608]{2,1,0:T(8,128)(2,1)S(1)} async-done(((bf16[16,8,4608]{2,1,0:T(8,128)(2,1)}), bf16[16,8,4608]{2,1,0:T(8,128)(2,1)S(1)}, u32[]{:S(2)}, u32[]{:S(2)}) %all-to-all-start) | async-done | bytes 1179680 | tf_op jit(solution)/shard_map/all_to_all | solution.py:44
  43.9 1.1 convolution_convert_fusion
  44.9 1.5 reshape.70
  46.5 0.6 fusion.10
  47.2 1.4 all_to_all.24
  48.6 11.1 %all-to-all-start.1 = ((f32[32,1,2560]{2,1,0:T(1,128)}), f32[32,1,2560]{2,1,0:T(1,128)S(1)}, u32[]{:S(2)}, u32[]{:S(2)}) async-start(f32[32,1,2560]{2,1,0:T(1,128)} %all_to_all.24), calls=%async_computation.1 | async-start | bytes 655360 | tf_op jit(solution)/shard_map/all_to_all | solution.py:53
  60.4 13.1 %all-to-all-done.1 = f32[32,1,2560]{2,1,0:T(1,128)S(1)} async-done(((f32[32,1,2560]{2,1,0:T(1,128)}), f32[32,1,2560]{2,1,0:T(1,128)S(1)}, u32[]{:S(2)}, u32[]{:S(2)}) %all-to-all-start.1) | async-done | bytes 327712 | tf_op jit(solution)/shard_map/all_to_all | solution.py:53
  73.5 0.8 reduce.1
  74.2 0.3 reshape.72
  74.9 0.2 copy.25
  75.2 0.2 convert_element_type.55
  75.4 0.2 fusion.5
  75.7 14.6 %all_to_all.30 = bf16[32,24,128]{2,1,0:T(8,128)(2,1)S(1)} all-to-all(bf16[32,24,128]{2,1,0:T(8,128)(2,1)S(1)} %bitcast.47), channel_id=1, replica_groups=mesh['dp'=16,'tensor'=32] {'tensor'}, dimensions={0} | all-to-all | bytes 393216 | tf_op jit(solution)/shard_map/all_to_all | solution.py:75
  90.2 4.3 %stack.2 = bf16[32,128,1024]{2,1,0:T(8,128)(2,1)} broadcast(bf16[128,1024]{1,0:T(8,128)(2,1)S(1)} %copy-done.4), dimensions={1,2} | broadcast | bytes 8650752 | tf_op jit(solution)/shard_map/stack | solution.py:35
  94.5 5.0 %all-to-all-start.4 = ((bf16[32,128,1024]{2,1,0:T(8,128)(2,1)}), bf16[32,128,1024]{2,1,0:T(8,128)(2,1)}, u32[]{:S(2)}, u32[]{:S(2)}) async-start(bf16[32,128,1024]{2,1,0:T(8,128)(2,1)} %stack.2), calls=%async_computation.4 | async-start | bytes 16777216 | tf_op jit(solution)/shard_map/all_to_all | solution.py:35
  99.7 0.4 convolution_multiply_fusion.1
  100.3 0.3 concatenate.18
  100.6 0.4 fusion.8
  101.1 1.5 fusion.1
  102.6 186.4 %all-to-all-done.4 = bf16[32,128,1024]{2,1,0:T(8,128)(2,1)} async-done(((bf16[32,128,1024]{2,1,0:T(8,128)(2,1)}), bf16[32,128,1024]{2,1,0:T(8,128)(2,1)}, u32[]{:S(2)}, u32[]{:S(2)}) %all-to-all-start.4) | async-done | bytes 8388640 | tf_op jit(solution)/shard_map/all_to_all | solution.py:35
  288.9 5.0 %all-to-all-start.3 = ((bf16[16,8,4608]{2,1,0:T(8,128)(2,1)}), bf16[16,8,4608]{2,1,0:T(8,128)(2,1)S(1)}, u32[]{:S(2)}, u32[]{:S(2)}) async-start(bf16[16,8,4608]{2,1,0:T(8,128)(2,1)} %fusion.1), calls=%async_computation.3 | async-start | bytes 2359296 | tf_op jit(solution)/shard_map/all_to_all | solution.py:93
  294.0 1.8 convolution_multiply_fusion
  295.8 5.9 %fusion.3 = bf16[4096,256]{1,0:T(8,128)(2,1)} fusion(f32[4096,256]{1,0:T(8,128)S(1)} %bitcast.40, bf16[4096,1024]{1,0:T(8,128)(2,1)} %bitcast.8, bf16[256,1024]{1,0:T(8,128)(2,1)S(1)} %copy-done.7, pred[4096]{0:T(1024)(128)(4,1)S(1)} %broadcast_bitcast_fusion), kind=kOutput, calls=%fused_computation.6 | convolution fusion | flops 2150629376 | bytes 15208448 | tf_op jit(solution)/shard_map/dot_general | solution.py:94
  301.7 22.8 %all-to-all-done.3 = bf16[16,8,4608]{2,1,0:T(8,128)(2,1)S(1)} async-done(((bf16[16,8,4608]{2,1,0:T(8,128)(2,1)}), bf16[16,8,4608]{2,1,0:T(8,128)(2,1)S(1)}, u32[]{:S(2)}, u32[]{:S(2)}) %all-to-all-start.3) | async-done | bytes 1179680 | tf_op jit(solution)/shard_map/all_to_all | solution.py:93
  324.5 0.2 reduce
  324.7 0.2 reshape.82
  324.9 0.6 slice.46
  325.5 0.6 slice.47
  (38 shorter events, 1.4 us)
Async XLA Ops:
  0.6 45.9 %copy-start = (bf16[4096,256]{1,0:T(8,128)(2,1)S(1)}, bf16[4096,256]{1,0:T(8,128)(2,1)}, u32[]{:S(2)}) copy-start(bf16[4096,256]{1,0:T(8,128)(2,1)} %param.8) | copy-start | bytes 6291460
  0.6 12.6 %copy-start.5 = (s32[512]{0:T(512)S(1)}, s32[512]{0:T(512)}, u32[]{:S(2)}) copy-start(s32[512]{0:T(512)} %param.13) | copy-start | bytes 6148
  0.7 12.6 %copy-start.6 = (s32[128]{0:T(128)S(1)}, s32[128]{0:T(128)}, u32[]{:S(2)}) copy-start(s32[128]{0:T(128)} %param.14) | copy-start | bytes 1540
  2.9 41.0 %all-to-all-start = ((bf16[16,8,4608]{2,1,0:T(8,128)(2,1)}), bf16[16,8,4608]{2,1,0:T(8,128)(2,1)S(1)}, u32[]{:S(2)}, u32[]{:S(2)}) async-start(bf16[16,8,4608]{2,1,0:T(8,128)(2,1)} %broadcast_in_dim.55), calls=%async_computation | async-start | bytes 2359296 | tf_op jit(solution)/shard_map/all_to_all | solution.py:44
  46.5 2.1 copy-start.1
  47.2 27.4 %copy-start.4 = (bf16[128,1024]{1,0:T(8,128)(2,1)S(1)}, bf16[128,1024]{1,0:T(8,128)(2,1)}, u32[]{:S(2)}) copy-start(bf16[128,1024]{1,0:T(8,128)(2,1)} %param.9) | copy-start | bytes 786436
  48.6 24.9 %all-to-all-start.1 = ((f32[32,1,2560]{2,1,0:T(1,128)}), f32[32,1,2560]{2,1,0:T(1,128)S(1)}, u32[]{:S(2)}, u32[]{:S(2)}) async-start(f32[32,1,2560]{2,1,0:T(1,128)} %all_to_all.24), calls=%async_computation.1 | async-start | bytes 655360 | tf_op jit(solution)/shard_map/all_to_all | solution.py:53
  94.5 194.4 %all-to-all-start.4 = ((bf16[32,128,1024]{2,1,0:T(8,128)(2,1)}), bf16[32,128,1024]{2,1,0:T(8,128)(2,1)}, u32[]{:S(2)}, u32[]{:S(2)}) async-start(bf16[32,128,1024]{2,1,0:T(8,128)(2,1)} %stack.2), calls=%async_computation.4 | async-start | bytes 16777216 | tf_op jit(solution)/shard_map/all_to_all | solution.py:35
  99.6 0.6 copy-start.2
  101.1 192.9 %copy-start.3 = (bf16[4,8,16,128]{3,2,1,0:T(8,128)(2,1)S(1)}, bf16[4,8,16,128]{3,2,1,0:T(8,128)(2,1)}, u32[]{:S(2)}) copy-start(bf16[4,8,16,128]{3,2,1,0:T(8,128)(2,1)} %copy-done.2) | copy-start | bytes 393220
  288.9 35.6 %all-to-all-start.3 = ((bf16[16,8,4608]{2,1,0:T(8,128)(2,1)}), bf16[16,8,4608]{2,1,0:T(8,128)(2,1)S(1)}, u32[]{:S(2)}, u32[]{:S(2)}) async-start(bf16[16,8,4608]{2,1,0:T(8,128)(2,1)} %fusion.1), calls=%async_computation.3 | async-start | bytes 2359296 | tf_op jit(solution)/shard_map/all_to_all | solution.py:93
  293.9 1.9 copy-start.7
